TPU v7x, 128 devices: a whole 4x4x4 slice. The times are simulated.
128 devices in a mesh: ctx: 16 (over y, x), grp: 8 (over z, core).
Axes of the slice: x: 4, y: 4, z: 4, core: 2. Of those that a mesh axis runs over, the one named last changes fastest.
Arguments:
- residual: bfloat16 [8, 2048, 2880], P('grp', 'ctx'), may hold values from -3 to 3
- queries: bfloat16 [8, 2048, 2048], P('grp', 'ctx'), may hold values from -8 to 8
- stretch_kv: bfloat16 [8, 2048, 1024], P('grp', 'ctx'), may hold values from -8 to 8
- cache_kv: bfloat16 [8, 4096, 1024], P('grp', 'ctx'), may hold values from -6 to 6
- doc_lengths: int32 [8, 8], P('grp'), may hold values from 1 to 3072, 6144 in all within a row
- sinks: float32 [32], replicated, may hold values from 2 to 6
- out_proj: bfloat16 [2048, 2880], P('ctx'), may hold values from -0.75 to 0.75
- norm_gain: float32 [2880], replicated, may hold values from 0.1 to 1.9
- router: bfloat16 [2880, 64], replicated, may hold values from -0.109375 to 0.109375
- expert_ids: int32 [8, 2048, 4], P('grp', 'ctx'), may hold values from 0 to 63, all different within a row; in each aligned block of 128 rows (0 to 127, 128 to 255, ..., all dimensions but the last counted through in order) at most 10 rows name the same one
- expert_in: bfloat16 [128, 2880, 1536], P(('ctx', 'grp')), may hold values from -0.109375 to 0.109375
- expert_out: bfloat16 [128, 768, 2880], P(('ctx', 'grp')), may hold values from -0.15625 to 0.15625
Outputs:
- resid_mid: bfloat16 [8, 2048, 2880], P('grp', 'ctx')
- layer_out: bfloat16 [8, 2048, 2880], P('grp', 'ctx')
Inputs may be any that keep to these rules, and one draw needn't show every extreme that they name: `expert_ids`: in the rows of one device (aligned blocks of 128 tokens, sequence after sequence), each expert is named by at most 10 rows, and in some blocks one expert by exactly 10; a token's 4 experts differ. `doc_lengths`: A sequence's 8 lengths sum to 6144; the longest is exactly 3072.
All inputs are finite; a program needn't handle non-finite values.
Results may differ from a plain program's by a relative error of at most 0.015.
Values may be sent and summed in bfloat16 or wider, within the bound.
No kernel may reach another device: no remote copies, remote signals or barrier semaphores. Data moves between devices by JAX's collectives and lax.ppermute only.
A program may use at most 128 MiB of HBM per device.

v0:
```python
import math

import jax
import jax.numpy as jnp
from jax import lax
from jax.experimental import pallas as pl
from jax.experimental.pallas import tpu as pltpu
from jax.sharding import PartitionSpec as P

HEADS = 32
KVH = 8
HD = 64
CACHE_TK = 256


def flash_all(qpad, qpos, qstart, sink_rows, kv_all, cache_rows, bounds, steps, scale):
    pairs, rows, lanes = qpad.shape
    tokens = qpos.shape[0]
    sources, span, width = kv_all.shape
    stretch_rows = span - cache_rows
    cache_steps = cache_rows // CACHE_TK
    n_cache = sources * cache_steps
    v_base = width // 2
    reps = rows // tokens

    def block_of(j, s):
        return jnp.minimum(s[0] + j, s[1])

    def kernel(s_ref, q_ref, qpos_ref, qstart_ref, sink_ref, c_ref, t_ref, o_ref, m_sc, l_sc, acc_sc):
        j = pl.program_id(0)
        b = s_ref[0] + j

        @pl.when(j == 0)
        def _():
            m_sc[...] = sink_ref[...]
            l_sc[...] = jnp.zeros_like(l_sc)
            acc_sc[...] = jnp.zeros_like(acc_sc)

        def step(kv_ref, first, count, masked):
            if masked:
                kpos = first + lax.broadcasted_iota(jnp.int32, (1, count), 1)
                allowed = ((kpos <= qpos_ref[...]) & (kpos >= qstart_ref[...]))[None]
            for p in range(pairs):
                keys = kv_ref[:, p * lanes:(p + 1) * lanes]
                values = kv_ref[:, v_base + p * lanes:v_base + (p + 1) * lanes]
                s = lax.dot_general(
                    q_ref[p], keys, (((1,), (1,)), ((), ())), preferred_element_type=jnp.float32
                ) * scale
                m_prev = m_sc[p]
                if masked:
                    s3 = s.reshape(reps, tokens, count)
                    top = jnp.max(jnp.where(allowed, s3, -jnp.inf), axis=2, keepdims=True).reshape(rows, 1)
                    m_new = jnp.maximum(m_prev, top)
                    e3 = jnp.exp(s3 - m_new.reshape(reps, tokens, 1))
                    w = jnp.where(allowed, e3, 0.0).reshape(rows, count)
                else:
                    m_new = jnp.maximum(m_prev, jnp.max(s, axis=1, keepdims=True))
                    w = jnp.exp(s - m_new)
                shrink = jnp.exp(m_prev - m_new)
                l_sc[p] = l_sc[p] * shrink + jnp.sum(w, axis=1, keepdims=True)
                acc_sc[p] = acc_sc[p] * shrink + jnp.dot(
                    w.astype(jnp.bfloat16), values, preferred_element_type=jnp.float32
                )
                m_sc[p] = m_new

        live = b <= s_ref[1]

        def branch(kv_ref, first, count):
            inside = (first >= s_ref[3]) & (first + count - 1 <= s_ref[2])

            @pl.when(inside)
            def _():
                step(kv_ref, first, count, False)

            @pl.when(jnp.logical_not(inside))
            def _():
                step(kv_ref, first, count, True)

        @pl.when(live & (b < n_cache))
        def _():
            branch(c_ref, b * CACHE_TK, CACHE_TK)

        @pl.when(live & (b >= n_cache))
        def _():
            branch(t_ref, sources * cache_rows + (b - n_cache) * stretch_rows, stretch_rows)

        @pl.when(j == pl.num_programs(0) - 1)
        def _():
            denom = l_sc[...] + jnp.exp(sink_ref[...] - m_sc[...])
            o_ref[...] = (acc_sc[...] / denom).astype(o_ref.dtype)

    def cache_map(j, s):
        c = jnp.minimum(block_of(j, s), n_cache - 1)
        return (c // cache_steps, c % cache_steps, 0)

    def stretch_map(j, s):
        return (jnp.maximum(block_of(j, s) - n_cache, 0), cache_rows // stretch_rows, 0)

    grid_spec = pltpu.PrefetchScalarGridSpec(
        num_scalar_prefetch=1,
        grid=(steps,),
        in_specs=[
            pl.BlockSpec((pairs, rows, lanes), lambda j, s: (0, 0, 0)),
            pl.BlockSpec((tokens, 1), lambda j, s: (0, 0)),
            pl.BlockSpec((tokens, 1), lambda j, s: (0, 0)),
            pl.BlockSpec((pairs, rows, 1), lambda j, s: (0, 0, 0)),
            pl.BlockSpec((None, CACHE_TK, width), cache_map),
            pl.BlockSpec((None, stretch_rows, width), stretch_map),
        ],
        out_specs=pl.BlockSpec((pairs, rows, lanes), lambda j, s: (0, 0, 0)),
        scratch_shapes=[
            pltpu.VMEM((pairs, rows, 1), jnp.float32),
            pltpu.VMEM((pairs, rows, 1), jnp.float32),
            pltpu.VMEM((pairs, rows, lanes), jnp.float32),
        ],
    )
    keys = sources * span // 2
    return pl.pallas_call(
        kernel,
        grid_spec=grid_spec,
        out_shape=jax.ShapeDtypeStruct((pairs, rows, lanes), jnp.bfloat16),
        compiler_params=pltpu.CompilerParams(
            dimension_semantics=("arbitrary",), vmem_limit_bytes=48 * 1024 * 1024
        ),
        cost_estimate=pl.CostEstimate(
            flops=4 * pairs * rows * lanes * keys,
            transcendentals=pairs * rows * keys,
            bytes_accessed=kv_all.size + 4 * qpad.size,
        ),
    )(bounds, qpad, qpos, qstart, sink_rows, kv_all, kv_all)


def block_index(position, sources, cache_rows, stretch_rows):
    cache_end = sources * cache_rows
    return jnp.where(
        position < cache_end,
        position // CACHE_TK,
        sources * (cache_rows // CACHE_TK) + (position - cache_end) // stretch_rows,
    )


def attention(queries_local, kv_all, cache_rows, sinks, query_pos, query_start, longest):
    tokens = queries_local.shape[0]
    groups = HEADS // KVH
    pairs = KVH // 2
    sources, span, _ = kv_all.shape
    stretch_rows = span - cache_rows
    q6 = queries_local.reshape(tokens, pairs, 2, groups, HD).transpose(1, 2, 3, 0, 4)
    zeros = jnp.zeros_like(q6[:, 0])
    qpad = jnp.stack(
        [jnp.concatenate([q6[:, 0], zeros], axis=-1), jnp.concatenate([zeros, q6[:, 1]], axis=-1)], axis=1
    ).reshape(pairs, 2 * groups * tokens, 2 * HD)
    rows = 2 * groups * tokens
    sink_rows = jnp.repeat(sinks.reshape(pairs, 2 * groups), tokens, axis=1).reshape(pairs, rows, 1)
    first = block_index(query_start[0], sources, cache_rows, stretch_rows)
    last = block_index(query_pos[-1], sources, cache_rows, stretch_rows)
    bounds = jnp.stack([first, last, query_pos[0], query_start[-1]]).astype(jnp.int32)
    cache_end = sources * cache_rows

    def static_block(position):
        if position < cache_end:
            return position // CACHE_TK
        return sources * (cache_rows // CACHE_TK) + (position - cache_end) // stretch_rows

    steps = 1
    for device in range(sources):
        low_q = cache_end + device * tokens
        high_q = low_q + tokens - 1
        low = max(0, low_q - longest + 1)
        blocks = static_block(high_q) - static_block(low) + 1
        steps = max(steps, blocks)
    out = flash_all(
        qpad, query_pos.reshape(tokens, 1), query_start.reshape(tokens, 1), sink_rows, kv_all, cache_rows,
        bounds, steps, 1.0 / math.sqrt(HD),
    )
    o6 = out.reshape(pairs, 2, groups, tokens, 2, HD)
    picked = jnp.stack([o6[:, 0, :, :, 0], o6[:, 1, :, :, 1]], axis=1)
    return picked.transpose(3, 0, 1, 2, 4).reshape(tokens, HEADS * HD)


def doc_index(positions, lengths):
    ends = jnp.cumsum(lengths)
    return jnp.sum((positions[:, None] >= ends[None, :]).astype(jnp.int32), axis=1)


def gated_act(pre, half_width):
    gate = pre[:, :half_width]
    upper = pre[:, half_width:]
    return ((upper + 1.0) * gate * jax.nn.sigmoid(1.702 * gate)).astype(jnp.bfloat16)


def body(
    residual,
    queries,
    stretch_kv,
    cache_kv,
    doc_lengths,
    sinks,
    out_proj,
    norm_gain,
    router,
    expert_ids,
    expert_in,
    expert_out,
):
    tokens = residual.shape[1]
    width = residual.shape[2]
    cache_rows = cache_kv.shape[1]
    kv_cols = stretch_kv.shape[2] // 2
    groups = HEADS // KVH
    ctx_count = lax.axis_size("ctx")
    ctx_here = lax.axis_index("ctx")
    stretch_base = cache_rows * ctx_count
    span = cache_rows + tokens
    query_pos = stretch_base + ctx_here * tokens + jnp.arange(tokens, dtype=jnp.int32)
    lengths = doc_lengths[0]
    ends = jnp.cumsum(lengths)
    query_start = jnp.max(
        jnp.where(ends[None, :] <= query_pos[:, None], ends[None, :], 0), axis=1
    ).astype(jnp.int32)
    local_kv = jnp.concatenate([cache_kv[0], stretch_kv[0]], axis=0)
    kv_all = lax.all_gather(local_kv, "ctx", axis=0, tiled=False)
    attended = attention(queries[0], kv_all, cache_rows, sinks, query_pos, query_start, span * ctx_count // 2)
    grp_here = lax.axis_index("grp")
    parity = grp_here % 2
    grp_count = lax.axis_size("grp")
    pair_perm = [(g, g ^ 1) for g in range(grp_count)]
    head_rows = out_proj.shape[0] // 2
    proj_half = lax.all_gather(
        lax.dynamic_slice_in_dim(out_proj, parity * head_rows, head_rows, 0), "ctx", axis=0, tiled=True
    )
    by_parity = attended.reshape(tokens, HEADS // 2, 2, HD)
    mine = jnp.where(parity == 0, by_parity[:, :, 0], by_parity[:, :, 1]).reshape(tokens, -1)
    theirs_cols = jnp.where(parity == 0, by_parity[:, :, 1], by_parity[:, :, 0]).reshape(tokens, -1)
    partner_cols = lax.ppermute(theirs_cols, "grp", pair_perm)
    both = jnp.dot(
        jnp.concatenate([mine, partner_cols], axis=0), proj_half, preferred_element_type=jnp.float32
    )
    back = lax.ppermute(both[tokens:], "grp", pair_perm)
    projected = both[:tokens] + back
    mid = (residual[0].astype(jnp.float32) + projected).astype(jnp.bfloat16)
    mid_float = mid.astype(jnp.float32)
    normed = (
        mid_float
        * lax.rsqrt(jnp.mean(mid_float * mid_float, axis=-1, keepdims=True) + 1e-05)
        * norm_gain
    ).astype(jnp.bfloat16)
    logits = jnp.dot(normed, router, preferred_element_type=jnp.float32)
    experts = router.shape[1]
    chosen_ids = expert_ids[0]
    topk = chosen_ids.shape[1]
    picks = chosen_ids[:, :, None] == jnp.arange(experts, dtype=jnp.int32)[None, None, :]
    chosen = jnp.sum(jnp.where(picks, logits[:, None, :], 0.0), axis=-1)
    raised = jnp.exp(chosen)
    route_weights = raised / jnp.sum(raised, axis=-1, keepdims=True)
    capacity = 2 * ((5 * tokens * topk + 8 * experts - 1) // (8 * experts))
    owners = 2 * experts
    half_cap = capacity // 2
    flat_ids = chosen_ids.reshape(-1)
    pairs = flat_ids.shape[0]
    onehot = (flat_ids[:, None] == jnp.arange(experts, dtype=jnp.int32)[None, :]).astype(jnp.int32)
    slots = jnp.sum(onehot * (jnp.cumsum(onehot, axis=0) - 1), axis=1)
    dest = (slots % half_cap) * owners + 2 * flat_ids + slots // half_cap
    source_rows = jnp.arange(pairs, dtype=jnp.int32) // topk
    placed = jnp.any(
        dest.reshape(tokens, topk)[:, :, None] == jnp.arange(owners * half_cap, dtype=jnp.int32)[None, None, :],
        axis=1,
    ).astype(jnp.bfloat16)
    split = (
        jnp.einsum("tso,tw->osw", placed.reshape(tokens, half_cap, owners), normed, preferred_element_type=jnp.float32)
        .astype(jnp.bfloat16)
        .transpose(1, 0, 2)
    )
    in_weights = expert_in[0]
    out_weights = expert_out[0]
    half_width = out_weights.shape[0]
    received = lax.all_to_all(split, ("ctx", "grp"), split_axis=1, concat_axis=1, tiled=True)
    partner_rows = lax.ppermute(received, "grp", pair_perm)

    def expert_half(rows):
        pre = jnp.einsum("sow,wh->soh", rows, in_weights, preferred_element_type=jnp.float32)
        gate = pre[..., :half_width]
        upper = pre[..., half_width:]
        hidden = ((upper + 1.0) * gate * jax.nn.sigmoid(1.702 * gate)).astype(jnp.bfloat16)
        return jnp.einsum("soh,hw->sow", hidden, out_weights, preferred_element_type=jnp.float32).astype(
            jnp.bfloat16
        )

    own_part = expert_half(received)
    partner_part = expert_half(partner_rows)
    partner_back = lax.ppermute(partner_part, "grp", pair_perm)
    summed = (own_part.astype(jnp.float32) + partner_back.astype(jnp.float32)).astype(jnp.bfloat16)
    returned = lax.all_to_all(summed, ("ctx", "grp"), split_axis=1, concat_axis=1, tiled=True)
    order_dest = dest.reshape(tokens, topk).T.reshape(-1)
    picks = (order_dest[:, None] == jnp.arange(owners * half_cap, dtype=jnp.int32)[None, :]).astype(jnp.bfloat16)
    chosen_rows = jnp.einsum(
        "rso,sow->rw", picks.reshape(-1, half_cap, owners), returned, preferred_element_type=jnp.float32
    ).reshape(topk, tokens, width)
    mixture = mid_float
    for k in range(topk):
        mixture = mixture + chosen_rows[k] * route_weights[:, k:k + 1]
    final = mixture.astype(jnp.bfloat16)
    return (mid[None], final[None])


def solution(mesh):
    return jax.shard_map(
        body,
        mesh=mesh,
        in_specs=(
            P("grp", "ctx", None),
            P("grp", "ctx", None),
            P("grp", "ctx", None),
            P("grp", "ctx", None),
            P("grp", None),
            P(),
            P("ctx", None),
            P(),
            P(),
            P("grp", "ctx", None),
            P(("ctx", "grp"), None, None),
            P(("ctx", "grp"), None, None),
        ),
        out_specs=(P("grp", "ctx", None), P("grp", "ctx", None)),
        check_vma=False,
    )
```

profile of v0, /device:TPU:1, one launch (start us, length us, event | category | flops | bytes accessed | tf_op | source)
XLA Modules:
  0.0 432.6 jit_solution(2858355862535357036)
XLA Ops:
  7.2 2.1 pad_maximum_fusion.1
  9.7 1.0 copy.101
  19.6 0.7 copy.76
  20.5 2.0 reshape_reshape.8.sink_ref
  22.5 1.3 pad_add_fusion.s_ref
  23.8 79.4 %all-gather.6.cloned.1.call-done = bf16[6144,1024]{1,0:T(8,128)(2,1)} async-done(((bf16[384,1024]{1,0:T(8,128)(2,1)}), bf16[6144,1024]{1,0:T(8,128)(2,1)}) %all-gather.6.cloned.1.call-update) | async-done | bytes 12582928 | tf_op jit(solution)/shard_map/all_gather | solution.py:222
  103.3 29.0 %shard_map.131 = bf16[4,1024,128]{2,1,0:T(8,128)(2,1)S(1)} custom-call(s32[4]{0:T(128)S(1)} %pad_add_fusion.s_ref, bf16[4,1024,128]{2,1,0:T(8,128)(2,1)S(1)} %bitcast.94, s32[128,1]{1,0:T(8,128)S(1)} %iota_add_fusion.qpos_ref, s32[128,1]{1,0:T(8,128)S(1)} %copy.77.qstart_ref, f32[4,1024,1]{2,1,0:T(8,128)S(1)} %reshape_reshape.8.sink_ref, ...), custom_call_target="tpu_custom_call" | custom-call | flops 6442450944 | bytes 8388608 | tf_op jit(solution)/shard_map/pallas_call | solution.py:118
  132.2 1.0 copy-done.2
  133.2 1.5 copy.79
  134.7 0.8 reshape.165
  136.2 30.7 %collective-permute-start = (bf16[128,1024]{0,1:T(8,128)(2,1)S(1)}, bf16[128,1024]{0,1:T(8,128)(2,1)S(1)}, u32[]{:S(2)}, u32[]{:S(2)}) collective-permute-start(bf16[128,1024]{0,1:T(8,128)(2,1)S(1)} %bitcast.106), channel_id=1, source_target_pairs={{0,1},{1,0},{2,3},{3,2},{4,5},{5,4},{6,7},{7,6},{8,9},{9,8},{10,11... | collective-permute-start | bytes 786440 | tf_op jit(solution)/shard_map/ppermute | solution.py:235
  166.9 1.2 collective-permute-done
  168.1 5.3 %fusion.36 = f32[256,2880]{0,1:T(8,128)S(1)} fusion(bf16[1024,2880]{1,0:T(8,128)(2,1)} %all-gather.4.cloned.1.call-done, bf16[128,1024]{0,1:T(8,128)(2,1)S(1)} %collective-permute-done, bf16[128,1024]{0,1:T(8,128)(2,1)S(1)} %bitcast.105), kind=kOutput, calls=%fused_computation.51 | convolution fusion | flops 1510998016 | bytes 9371648 | tf_op jit(solution)/shard_map/dot_general | solution.py:236
  173.4 1.6 copy-done.5
  175.0 1.2 slice.117
  176.9 1.2 reduce-window.19
  179.6 2.0 fusion.15
  181.6 3.1 convolution_convert_fusion
  184.7 8.3 %copy.92 = bf16[5,128,2880]{2,0,1:T(8,128)(2,1)} copy(bf16[5,128,2880]{1,2,0:T(8,128)(2,1)} %convolution_convert_fusion) | data formatting | bytes 7372800 | tf_op jit(solution)/shard_map/convert_element_type | solution.py:271
  193.0 95.7 %all_to_all.10 = bf16[5,128,2880]{2,0,1:T(8,128)(2,1)} all-to-all(bf16[5,128,2880]{2,0,1:T(8,128)(2,1)} %copy.92), channel_id=1, replica_groups=mesh['ctx'=16,'grp'=8] {'ctx','grp'}, dimensions={1} | all-to-all | bytes 7372800 | tf_op jit(solution)/shard_map/all_to_all | solution.py:277
  288.7 7.9 %copy.93 = bf16[5,128,2880]{1,2,0:T(8,128)(2,1)} copy(bf16[5,128,2880]{2,0,1:T(8,128)(2,1)} %all_to_all.10) | data formatting | bytes 7372800 | tf_op jit(solution)/shard_map/all_to_all | solution.py:277
  296.6 1.3 collective-permute-start.2
  297.9 6.3 %collective-permute-done.2 = bf16[5,128,2880]{1,2,0:T(8,128)(2,1)S(1)} collective-permute-done((bf16[5,128,2880]{1,2,0:T(8,128)(2,1)}, bf16[5,128,2880]{1,2,0:T(8,128)(2,1)S(1)}, u32[]{:S(2)}, u32[]{:S(2)}) %collective-permute-start.2) | collective-permute-done | bytes 3686432 | tf_op jit(solution)/shard_map/ppermute | solution.py:278
  304.2 9.5 %fusion = f32[5,128,1536]{2,1,0:T(8,128)S(1)} fusion(bf16[5,128,2880]{1,2,0:T(8,128)(2,1)S(1)} %collective-permute-done.2, bf16[1,2880,1536]{2,1,0:T(8,128)(2,1)} %param.22), kind=kOutput, calls=%fused_computation | convolution fusion | flops 5662310400 | bytes 16465920 | tf_op jit(solution)/shard_map/sow,wh->soh/dot_general | solution.py:281
  313.7 5.9 %convolution_convert_fusion.1 = bf16[5,128,2880]{1,2,0:T(8,128)(2,1)S(1)} fusion(bf16[1,768,2880]{1,2,0:T(8,128)(2,1)} %param.23, f32[5,128,1536]{2,1,0:T(8,128)S(1)} %fusion), kind=kOutput, calls=%fused_computation.7 | convolution fusion | flops 2836930560 | bytes 12042240 | tf_op jit(solution)/shard_map/soh,hw->sow/dot_general | solution.py:285
  320.1 6.3 %fusion.2 = f32[5,128,1536]{2,1,0:T(8,128)S(1)} fusion(bf16[5,128,2880]{1,2,0:T(8,128)(2,1)S(1)} %copy-done.4, bf16[1,2880,1536]{2,1,0:T(8,128)(2,1)S(1)} %bitcast.110), kind=kOutput, calls=%fused_computation.2 | convolution fusion | flops 5662310400 | bytes 16465920 | tf_op jit(solution)/shard_map/sow,wh->soh/dot_general | solution.py:281
  326.4 5.5 %add_convert_fusion = bf16[5,128,2880]{1,2,0:T(8,128)(2,1)} fusion(bf16[5,128,2880]{1,2,0:T(8,128)(2,1)S(1)} %collective-permute-done.3, bf16[1,768,2880]{1,2,0:T(8,128)(2,1)S(1)} %bitcast.112, f32[5,128,1536]{2,1,0:T(8,128)S(1)} %fusion.2), kind=kOutput, calls=%fused_computation.4 | convolution fusion | flops 2844303360 | bytes 15728640 | tf_op jit(solution)/shard_map/soh,hw->sow/dot_general | solution.py:285
  331.9 8.3 %copy.95 = bf16[5,128,2880]{2,0,1:T(8,128)(2,1)} copy(bf16[5,128,2880]{1,2,0:T(8,128)(2,1)} %add_convert_fusion) | data formatting | bytes 7372800 | tf_op jit(solution)/shard_map/convert_element_type | solution.py:292
  340.2 4.9 %all-to-all-start.1 = ((bf16[5,128,2880]{2,0,1:T(8,128)(2,1)}), bf16[5,128,2880]{2,0,1:T(8,128)(2,1)}, u32[]{:S(2)}, u32[]{:S(2)}) async-start(bf16[5,128,2880]{2,0,1:T(8,128)(2,1)} %copy.95), calls=%async_computation.1 | async-start | bytes 12058624 | tf_op jit(solution)/shard_map/all_to_all | solution.py:293
  345.9 72.8 %all-to-all-done.1 = bf16[5,128,2880]{2,0,1:T(8,128)(2,1)} async-done(((bf16[5,128,2880]{2,0,1:T(8,128)(2,1)}), bf16[5,128,2880]{2,0,1:T(8,128)(2,1)}, u32[]{:S(2)}, u32[]{:S(2)}) %all-to-all-start.1) | async-done | bytes 3686432 | tf_op jit(solution)/shard_map/all_to_all | solution.py:293
  418.8 5.3 %convolution_bitcast_fusion = f32[512,2880]{0,1:T(8,128)S(1)} fusion(bf16[5,128,2880]{2,0,1:T(8,128)(2,1)} %all-to-all-done.1, s32[5,128]{1,0:T(8,128)S(1)} %multiply_add_fusion, s32[512]{0:T(512)S(1)} %bitcast.108), kind=kOutput, calls=%fused_computation.5 | convolution fusion | flops 1887764480 | bytes 9589248 | tf_op jit(solution)/shard_map/rso,sow->rw/dot_general | solution.py:296
  424.1 1.4 fusion.33
  (86 shorter events, 6.5 us)
Async XLA Ops:
  7.2 2.3 copy-start
  7.2 96.1 %all-gather.6.cloned.1.call-start = ((), (), s32[]{:S(2)}) async-start(), calls=%async_computation.3 | async-start | bytes 13369344 | tf_op jit(solution)/shard_map/all_gather | solution.py:222
  9.4 1.4 copy-start.11
  9.4 9.6 %copy-start.6 = (bf16[1,128,2048]{2,1,0:T(8,128)(2,1)S(1)}, bf16[1,128,2048]{2,1,0:T(8,128)(2,1)}, u32[]{:S(2)}) copy-start(bf16[1,128,2048]{2,1,0:T(8,128)(2,1)} %param.13) | copy-start | bytes 1572868
  9.4 157.5 %all-gather.4.cloned.1.call-start = ((), (), s32[]{:S(2)}) async-start(), calls=%async_computation.2 | async-start | bytes 6406144 | tf_op jit(solution)/shard_map/all_gather | solution.py:229
  19.5 0.9 copy-start.9
  132.2 1.0 copy-start.2
  136.2 31.9 %collective-permute-start = (bf16[128,1024]{0,1:T(8,128)(2,1)S(1)}, bf16[128,1024]{0,1:T(8,128)(2,1)S(1)}, u32[]{:S(2)}, u32[]{:S(2)}) collective-permute-start(bf16[128,1024]{0,1:T(8,128)(2,1)S(1)} %bitcast.106), channel_id=1, source_target_pairs={{0,1},{1,0},{2,3},{3,2},{4,5},{5,4},{6,7},{7,6},{8,9},{9,8},{10,11... | collective-permute-start | bytes 786440 | tf_op jit(solution)/shard_map/ppermute | solution.py:235
  173.4 1.6 copy-start.5
  175.0 1.6 copy-start.8
  176.2 3.5 collective-permute-start.1
  179.4 2.2 copy-start.7
  181.6 242.5 %copy-start.3 = (bf16[128,2880]{0,1:T(8,128)(2,1)}, bf16[128,2880]{0,1:T(8,128)(2,1)S(1)}, u32[]{:S(2)}) copy-start(bf16[128,2880]{0,1:T(8,128)(2,1)S(1)} %get-tuple-element.3) | copy-start | bytes 2211844
  296.6 7.5 %collective-permute-start.2 = (bf16[5,128,2880]{1,2,0:T(8,128)(2,1)}, bf16[5,128,2880]{1,2,0:T(8,128)(2,1)S(1)}, u32[]{:S(2)}, u32[]{:S(2)}) collective-permute-start(bf16[5,128,2880]{1,2,0:T(8,128)(2,1)} %copy.93), channel_id=1, source_target_pairs={{0,1},{1,0},{2,3},{3,2},{4,5},{5,4},{6,7},{7,6},{8,9},{9,8},{10,11... | collective-permute-start | bytes 11059208 | tf_op jit(solution)/shard_map/ppermute | solution.py:278
  304.1 15.9 %slice-start = ((s8[8847360]{0:T(1024)(128)(4,1)}), s8[4194304]{0:T(1024)(128)(4,1)S(1)}, s32[]{:S(2)}) async-start(s8[8847360]{0:T(1024)(128)(4,1)} %bitcast.109), calls=%async_computation.4 | async-start | bytes 8388608
  304.2 15.9 %slice-start.1 = ((s8[8847360]{0:T(1024)(128)(4,1)}), s8[4194304]{0:T(1024)(128)(4,1)S(1)}, s32[]{:S(2)}) async-start(s8[8847360]{0:T(1024)(128)(4,1)} %bitcast.109), calls=%async_computation.5 | async-start | bytes 8388608
  304.2 22.3 %slice-start.3 = ((s8[4423680]{0:T(1024)(128)(4,1)}), s8[4194304]{0:T(1024)(128)(4,1)S(1)}, s32[]{:S(2)}) async-start(s8[4423680]{0:T(1024)(128)(4,1)} %bitcast.111), calls=%async_computation.7 | async-start | bytes 8388608
  313.6 6.4 %copy-start.4 = (bf16[5,128,2880]{1,2,0:T(8,128)(2,1)S(1)}, bf16[5,128,2880]{1,2,0:T(8,128)(2,1)}, u32[]{:S(2)}) copy-start(bf16[5,128,2880]{1,2,0:T(8,128)(2,1)} %copy.93) | copy-start | bytes 11059204
  313.7 6.4 %slice-start.2 = ((s8[8847360]{0:T(1024)(128)(4,1)}), s8[458752]{0:T(1024)(128)(4,1)S(1)}, s32[]{:S(2)}) async-start(s8[8847360]{0:T(1024)(128)(4,1)} %bitcast.109), calls=%async_computation.6 | async-start | bytes 917504
  313.7 12.7 %slice-start.4 = ((s8[4423680]{0:T(1024)(128)(4,1)}), s8[229376]{0:T(1024)(128)(4,1)S(1)}, s32[]{:S(2)}) async-start(s8[4423680]{0:T(1024)(128)(4,1)} %bitcast.111), calls=%async_computation.8 | async-start | bytes 458752
  319.6 6.8 %collective-permute-start.3 = (bf16[5,128,2880]{1,2,0:T(8,128)(2,1)S(1)}, bf16[5,128,2880]{1,2,0:T(8,128)(2,1)S(1)}, u32[]{:S(2)}, u32[]{:S(2)}) collective-permute-start(bf16[5,128,2880]{1,2,0:T(8,128)(2,1)S(1)} %convolution_convert_fusion.1), channel_id=1, source_target_pairs={{0,1},{1,0},{2,3},{3,2},{4,5},{5,4},{6,7},{7,6},{8,9},{9,8},{10,11... | collective-permute-start | bytes 11059208 | tf_op jit(solution)/shard_map/ppermute | solution.py:291
  340.2 5.0 %copy-start.10 = (bf16[2880,64]{0,1:T(8,128)(2,1)S(1)}, bf16[2880,64]{0,1:T(8,128)(2,1)}, u32[]{:S(2)}) copy-start(bf16[2880,64]{0,1:T(8,128)(2,1)} %param.20) | copy-start | bytes 1105924
  340.2 78.6 %all-to-all-start.1 = ((bf16[5,128,2880]{2,0,1:T(8,128)(2,1)}), bf16[5,128,2880]{2,0,1:T(8,128)(2,1)}, u32[]{:S(2)}, u32[]{:S(2)}) async-start(bf16[5,128,2880]{2,0,1:T(8,128)(2,1)} %copy.95), calls=%async_computation.1 | async-start | bytes 12058624 | tf_op jit(solution)/shard_map/all_to_all | solution.py:293
  424.1 1.4 copy-start.1
Sparse Core Ops, SparseCore 0:
  10.2 93.0 all-gather.5
  106.0 59.6 all-gather.3
where the time goes:
time: 437 us; the launch traced here: 433 us
  waiting for transfers between devices  160 us (37%)
  blocking collectives  95.7 us (22%)
  matrix products  41.4 us (9%)
  starting transfers between devices  37.8 us (9%)
  local copies, waits for them, and re-layouts  37.5 us (9%)
  Pallas kernels  29 us (7%)
  between operations  21.9 us (5%)
  other arithmetic  9.39 us (2%)
    all_to_all x1, blocking collectives, body(): lax.all_to_all(split, ('ctx', 'grp'), split_axis=1, concat_axis=1, tiled=...  95.7 us
    all_gather x1, waiting for transfers between devices, body(): kv_all = lax.all_gather(local_kv, 'ctx', axis=0, tiled=False)  79.4 us
    all_to_all x1, waiting for transfers between devices, body(): lax.all_to_all(summed, ('ctx', 'grp'), split_axis=1, concat_axis=1, tiled...  72.8 us
    ppermute x1, starting transfers between devices, body(): partner_cols = lax.ppermute(theirs_cols, 'grp', pair_perm)  30.7 us
    pallas_call x1, Pallas kernels, flash_all(): pl.pallas_call(kernel, grid_spec=grid_spec, out_shape=jax.ShapeDtypeStruc...  29 us
    dot_general x2, matrix products, expert_half(): jnp.einsum('sow,wh->soh', rows, in_weights, preferred_element_type=jnp.fl...  15.8 us
    dot_general x2, matrix products, expert_half(): jnp.einsum('soh,hw->sow', hidden, out_weights, preferred_element_type=jnp...  11.3 us
  transfers between devices with their start and end apart: 7, of which 5 were waited for; matrix products, arithmetic and copies ran while one was open for 5% of the time, Pallas kernels for 7%

commit v1 on v0

--- a/solution.py
+++ b/solution.py
@@ -286,9 +286,22 @@
             jnp.bfloat16
         )
 
-    own_part = expert_half(received)
-    partner_part = expert_half(partner_rows)
+    def expert_hidden(rows):
+        pre = jnp.einsum("sow,wh->soh", rows, in_weights, preferred_element_type=jnp.float32)
+        gate = pre[..., :half_width]
+        upper = pre[..., half_width:]
+        return ((upper + 1.0) * gate * jax.nn.sigmoid(1.702 * gate)).astype(jnp.bfloat16)
+
+    def expert_down(hidden):
+        return jnp.einsum("soh,hw->sow", hidden, out_weights, preferred_element_type=jnp.float32).astype(
+            jnp.bfloat16
+        )
+
+    own_hidden = expert_hidden(received)
+    own_hidden, partner_rows = lax.optimization_barrier((own_hidden, partner_rows))
+    partner_part = expert_down(expert_hidden(partner_rows))
     partner_back = lax.ppermute(partner_part, "grp", pair_perm)
+    own_part = lax.optimization_barrier(expert_down(own_hidden))
     summed = (own_part.astype(jnp.float32) + partner_back.astype(jnp.float32)).astype(jnp.bfloat16)
     returned = lax.all_to_all(summed, ("ctx", "grp"), split_axis=1, concat_axis=1, tiled=True)
     order_dest = dest.reshape(tokens, topk).T.reshape(-1)

time: 437 us -> 434 us (level)
  starting transfers between devices: 37.8 us -> 7.22 us
  Pallas kernels: 29 us -> 46.1 us
  waiting for transfers between devices: 160 us -> 167 us
    ppermute x1, starting transfers between devices: 30.7 us -> 0.09 us  [body(): partner_cols = lax.ppermute(theirs_cols, 'grp', pair_perm)]
    pallas_call x1, Pallas kernels: 29 us -> 46.1 us  [flash_all(): pl.pallas_call(kernel, grid_spec=grid_spec, out_shape=jax.ShapeDtypeStruc...]
    all_gather x1, waiting for transfers between devices: 0.01 us -> 12.3 us  [body(): lax.all_gather(lax.dynamic_slice_in_dim(out_proj, parity * head_rows, hea...]
    ppermute x1, waiting for transfers between devices: 6.27 us -> 0.01 us  [body(): partner_rows = lax.ppermute(received, 'grp', pair_perm)]
  transfers between devices with their start and end apart: 7 -> 7, of which waited for: 5 -> 5; matrix products, arithmetic and copies ran while one was open for 5% -> 7% of each run, Pallas kernels for 7% -> 11%
where the time goes in v1:
time: 434 us; the launch traced here: 433 us
  waiting for transfers between devices  167 us (38%)
  blocking collectives  98.1 us (23%)
  Pallas kernels  46.1 us (11%)
  matrix products  41.9 us (10%)
  local copies, waits for them, and re-layouts  37.4 us (9%)
  between operations  21.9 us (5%)
  other arithmetic  12.8 us (3%)
  starting transfers between devices  7.22 us (2%)
    all_to_all x1, blocking collectives, body(): lax.all_to_all(split, ('ctx', 'grp'), split_axis=1, concat_axis=1, tiled=...  98.1 us
    all_gather x1, waiting for transfers between devices, body(): kv_all = lax.all_gather(local_kv, 'ctx', axis=0, tiled=False)  79.4 us
    all_to_all x1, waiting for transfers between devices, body(): lax.all_to_all(summed, ('ctx', 'grp'), split_axis=1, concat_axis=1, tiled...  72.9 us
    pallas_call x1, Pallas kernels, flash_all(): pl.pallas_call(kernel, grid_spec=grid_spec, out_shape=jax.ShapeDtypeStruc...  46.1 us
    dot_general x2, matrix products, expert_hidden(): jnp.einsum('sow,wh->soh', rows, in_weights, preferred_element_type=jnp.fl...  19.7 us
    all_gather x1, waiting for transfers between devices, body(): lax.all_gather(lax.dynamic_slice_in_dim(out_proj, parity * head_rows, hea...  12.3 us
  transfers between devices with their start and end apart: 7, of which 5 were waited for; matrix products, arithmetic and copies ran while one was open for 7% of the time, Pallas kernels for 11%

profile of v1, /device:TPU:1, one launch (start us, length us, event | category | flops | bytes accessed | tf_op | source)
XLA Modules:
  0.0 432.6 jit_solution(18023077081457035473)
XLA Ops:
  7.2 2.1 pad_maximum_fusion.1
  9.7 1.0 copy.123
  20.5 2.0 reshape_reshape.8.sink_ref
  22.5 1.4 pad_add_fusion.s_ref
  23.9 79.4 %all-gather.6.cloned.1.call-done = bf16[6144,1024]{1,0:T(8,128)(2,1)} async-done(((bf16[384,1024]{1,0:T(8,128)(2,1)}), bf16[6144,1024]{1,0:T(8,128)(2,1)}) %all-gather.6.cloned.1.call-update) | async-done | bytes 12582928 | tf_op jit(solution)/shard_map/all_gather | solution.py:222
  103.3 46.1 %shard_map.131 = bf16[4,1024,128]{2,1,0:T(8,128)(2,1)S(1)} custom-call(s32[4]{0:T(128)S(1)} %pad_add_fusion.s_ref, bf16[4,1024,128]{2,1,0:T(8,128)(2,1)S(1)} %bitcast.93, s32[128,1]{1,0:T(8,128)S(1)} %iota_add_fusion.qpos_ref, s32[128,1]{1,0:T(8,128)S(1)} %copy.99.qstart_ref, f32[4,1024,1]{2,1,0:T(8,128)S(1)} %reshape_reshape.8.sink_ref, ...), custom_call_target="tpu_custom_call" | custom-call | flops 6442450944 | bytes 8388608 | tf_op jit(solution)/shard_map/pallas_call | solution.py:118
  149.4 1.0 copy-done.2
  150.3 1.5 copy.101
  151.8 0.8 reshape.165
  153.4 12.3 %all-gather.4.cloned.1.call-done = bf16[1024,2880]{1,0:T(8,128)(2,1)} async-done(((bf16[64,2880]{1,0:T(8,128)(2,1)}), bf16[1024,2880]{1,0:T(8,128)(2,1)}) %all-gather.4.cloned.1.call-update) | async-done | bytes 5898256 | tf_op jit(solution)/shard_map/all_gather | solution.py:229
  165.7 5.3 %fusion.31 = f32[256,2880]{0,1:T(8,128)S(1)} fusion(bf16[1024,2880]{1,0:T(8,128)(2,1)} %all-gather.4.cloned.1.call-done, bf16[128,1024]{0,1:T(8,128)(2,1)S(1)} %collective-permute-done, bf16[128,1024]{0,1:T(8,128)(2,1)S(1)} %bitcast.104), kind=kOutput, calls=%fused_computation.49 | convolution fusion | flops 1510998016 | bytes 9371648 | tf_op jit(solution)/shard_map/dot_general | solution.py:236
  171.0 1.6 copy-done.4
  172.6 1.2 slice.117
  173.8 0.7 collective-permute-start.1
  174.8 1.2 reduce-window.19
  177.6 2.0 fusion.13
  179.6 3.1 convolution_convert_fusion
  182.6 8.3 %copy.114 = bf16[5,128,2880]{2,0,1:T(8,128)(2,1)} copy(bf16[5,128,2880]{1,2,0:T(8,128)(2,1)} %convolution_convert_fusion) | data formatting | bytes 7372800 | tf_op jit(solution)/shard_map/convert_element_type | solution.py:271
  190.9 98.1 %all_to_all.10 = bf16[5,128,2880]{2,0,1:T(8,128)(2,1)} all-to-all(bf16[5,128,2880]{2,0,1:T(8,128)(2,1)} %copy.114), channel_id=1, replica_groups=mesh['ctx'=16,'grp'=8] {'ctx','grp'}, dimensions={1} | all-to-all | bytes 7372800 | tf_op jit(solution)/shard_map/all_to_all | solution.py:277
  289.0 7.8 %copy.115 = bf16[5,128,2880]{1,2,0:T(8,128)(2,1)} copy(bf16[5,128,2880]{2,0,1:T(8,128)(2,1)} %all_to_all.10) | data formatting | bytes 7372800 | tf_op jit(solution)/shard_map/all_to_all | solution.py:277
  296.8 1.3 collective-permute-start.2
  298.1 10.5 %fusion.2 = f32[5,128,1536]{2,1,0:T(8,128)S(1)} fusion(bf16[5,128,2880]{1,2,0:T(8,128)(2,1)} %copy.115, bf16[1,2880,1536]{2,1,0:T(8,128)(2,1)} %param.22), kind=kOutput, calls=%fused_computation.2 | convolution fusion | flops 5662310400 | bytes 16465920 | tf_op jit(solution)/shard_map/sow,wh->soh/dot_general | solution.py:290
  309.1 9.2 %fusion = f32[5,128,1536]{2,1,0:T(8,128)S(1)} fusion(bf16[5,128,2880]{1,2,0:T(8,128)(2,1)S(1)} %collective-permute-done.2, bf16[1,2880,1536]{2,1,0:T(8,128)(2,1)} %param.22), kind=kOutput, calls=%fused_computation | convolution fusion | flops 5662310400 | bytes 16465920 | tf_op jit(solution)/shard_map/sow,wh->soh/dot_general | solution.py:290
  318.4 4.1 convolution_convert_fusion.1
  322.6 3.9 convolution_convert_fusion.2
  326.5 2.5 collective-permute-done.3
  329.0 2.8 add_convert_fusion
  331.8 8.3 %copy.117 = bf16[5,128,2880]{2,0,1:T(8,128)(2,1)} copy(bf16[5,128,2880]{1,2,0:T(8,128)(2,1)} %add_convert_fusion) | data formatting | bytes 7372800 | tf_op jit(solution)/shard_map/convert_element_type | solution.py:305
  340.1 5.0 %all-to-all-start.1 = ((bf16[5,128,2880]{2,0,1:T(8,128)(2,1)}), bf16[5,128,2880]{2,0,1:T(8,128)(2,1)}, u32[]{:S(2)}, u32[]{:S(2)}) async-start(bf16[5,128,2880]{2,0,1:T(8,128)(2,1)} %copy.117), calls=%async_computation.1 | async-start | bytes 12058624 | tf_op jit(solution)/shard_map/all_to_all | solution.py:306
  346.0 72.9 %all-to-all-done.1 = bf16[5,128,2880]{2,0,1:T(8,128)(2,1)} async-done(((bf16[5,128,2880]{2,0,1:T(8,128)(2,1)}), bf16[5,128,2880]{2,0,1:T(8,128)(2,1)}, u32[]{:S(2)}, u32[]{:S(2)}) %all-to-all-start.1) | async-done | bytes 3686432 | tf_op jit(solution)/shard_map/all_to_all | solution.py:306
  418.9 5.3 %convolution_bitcast_fusion = f32[512,2880]{0,1:T(8,128)S(1)} fusion(bf16[5,128,2880]{2,0,1:T(8,128)(2,1)} %all-to-all-done.1, s32[5,128]{1,0:T(8,128)S(1)} %multiply_add_fusion, s32[512]{0:T(512)S(1)} %bitcast.107), kind=kOutput, calls=%fused_computation.5 | convolution fusion | flops 1887764480 | bytes 9589248 | tf_op jit(solution)/shard_map/rso,sow->rw/dot_general | solution.py:309
  424.2 1.4 fusion.28
  (79 shorter events, 7.0 us)
Async XLA Ops:
  7.2 2.3 copy-start
  7.2 96.1 %all-gather.6.cloned.1.call-start = ((), (), s32[]{:S(2)}) async-start(), calls=%async_computation.3 | async-start | bytes 13369344 | tf_op jit(solution)/shard_map/all_gather | solution.py:222
  9.3 1.4 copy-start.10
  9.3 9.6 %copy-start.5 = (bf16[1,128,2048]{2,1,0:T(8,128)(2,1)S(1)}, bf16[1,128,2048]{2,1,0:T(8,128)(2,1)}, u32[]{:S(2)}) copy-start(bf16[1,128,2048]{2,1,0:T(8,128)(2,1)} %param.13) | copy-start | bytes 1572868
  9.4 156.3 %all-gather.4.cloned.1.call-start = ((), (), s32[]{:S(2)}) async-start(), calls=%async_computation.2 | async-start | bytes 6406144 | tf_op jit(solution)/shard_map/all_gather | solution.py:229
  19.4 0.9 copy-start.8
  149.4 1.0 copy-start.2
  153.4 12.4 %collective-permute-start = (bf16[128,1024]{0,1:T(8,128)(2,1)S(1)}, bf16[128,1024]{0,1:T(8,128)(2,1)S(1)}, u32[]{:S(2)}, u32[]{:S(2)}) collective-permute-start(bf16[128,1024]{0,1:T(8,128)(2,1)S(1)} %bitcast.105), channel_id=1, source_target_pairs={{0,1},{1,0},{2,3},{3,2},{4,5},{5,4},{6,7},{7,6},{8,9},{9,8},{10,11... | collective-permute-start | bytes 786440 | tf_op jit(solution)/shard_map/ppermute | solution.py:235
  171.0 1.6 copy-start.4
  172.6 1.9 copy-start.7
  173.8 3.8 collective-permute-start.1
  177.4 2.2 copy-start.6
  179.5 244.7 %copy-start.3 = (bf16[128,2880]{0,1:T(8,128)(2,1)}, bf16[128,2880]{0,1:T(8,128)(2,1)S(1)}, u32[]{:S(2)}) copy-start(bf16[128,2880]{0,1:T(8,128)(2,1)S(1)} %get-tuple-element.7) | copy-start | bytes 2211844
  296.8 12.3 %collective-permute-start.2 = (bf16[5,128,2880]{1,2,0:T(8,128)(2,1)}, bf16[5,128,2880]{1,2,0:T(8,128)(2,1)S(1)}, u32[]{:S(2)}, u32[]{:S(2)}) collective-permute-start(bf16[5,128,2880]{1,2,0:T(8,128)(2,1)} %copy.115), channel_id=1, source_target_pairs={{0,1},{1,0},{2,3},{3,2},{4,5},{5,4},{6,7},{7,6},{8,9},{9,8},{10,11... | collective-permute-start | bytes 11059208 | tf_op jit(solution)/shard_map/ppermute | solution.py:278
  308.5 9.8 %slice-start = ((s8[4423680]{0:T(1024)(128)(4,1)}), s8[4194304]{0:T(1024)(128)(4,1)S(1)}, s32[]{:S(2)}) async-start(s8[4423680]{0:T(1024)(128)(4,1)} %bitcast.108), calls=%async_computation.4 | async-start | bytes 8388608
  309.1 9.2 %slice-start.1 = ((s8[4423680]{0:T(1024)(128)(4,1)}), s8[229376]{0:T(1024)(128)(4,1)S(1)}, s32[]{:S(2)}) async-start(s8[4423680]{0:T(1024)(128)(4,1)} %bitcast.108), calls=%async_computation.5 | async-start | bytes 458752
  322.5 6.5 %collective-permute-start.3 = (bf16[5,128,2880]{1,2,0:T(8,128)(2,1)S(1)}, bf16[5,128,2880]{1,2,0:T(8,128)(2,1)S(1)}, u32[]{:S(2)}, u32[]{:S(2)}) collective-permute-start(bf16[5,128,2880]{1,2,0:T(8,128)(2,1)S(1)} %convolution_convert_fusion.1), channel_id=1, source_target_pairs={{0,1},{1,0},{2,3},{3,2},{4,5},{5,4},{6,7},{7,6},{8,9},{9,8},{10,11... | collective-permute-start | bytes 11059208 | tf_op jit(solution)/shard_map/ppermute | solution.py:303
  340.1 5.2 %copy-start.9 = (bf16[2880,64]{0,1:T(8,128)(2,1)S(1)}, bf16[2880,64]{0,1:T(8,128)(2,1)}, u32[]{:S(2)}) copy-start(bf16[2880,64]{0,1:T(8,128)(2,1)} %param.20) | copy-start | bytes 1105924
  340.1 78.8 %all-to-all-start.1 = ((bf16[5,128,2880]{2,0,1:T(8,128)(2,1)}), bf16[5,128,2880]{2,0,1:T(8,128)(2,1)}, u32[]{:S(2)}, u32[]{:S(2)}) async-start(bf16[5,128,2880]{2,0,1:T(8,128)(2,1)} %copy.117), calls=%async_computation.1 | async-start | bytes 12058624 | tf_op jit(solution)/shard_map/all_to_all | solution.py:306
  424.2 1.4 copy-start.1
Sparse Core Ops, SparseCore 0:
  10.2 93.0 all-gather.5
  106.0 59.6 all-gather.3

commit v2 on v0

--- a/solution.py
+++ b/solution.py
@@ -291,14 +291,18 @@
     partner_back = lax.ppermute(partner_part, "grp", pair_perm)
     summed = (own_part.astype(jnp.float32) + partner_back.astype(jnp.float32)).astype(jnp.bfloat16)
     returned = lax.all_to_all(summed, ("ctx", "grp"), split_axis=1, concat_axis=1, tiled=True)
-    order_dest = dest.reshape(tokens, topk).T.reshape(-1)
-    picks = (order_dest[:, None] == jnp.arange(owners * half_cap, dtype=jnp.int32)[None, :]).astype(jnp.bfloat16)
-    chosen_rows = jnp.einsum(
-        "rso,sow->rw", picks.reshape(-1, half_cap, owners), returned, preferred_element_type=jnp.float32
-    ).reshape(topk, tokens, width)
-    mixture = mid_float
-    for k in range(topk):
-        mixture = mixture + chosen_rows[k] * route_weights[:, k:k + 1]
+    slot_ids = jnp.arange(owners * half_cap, dtype=jnp.int32)
+    placed_weights = jnp.sum(
+        jnp.where(dest.reshape(tokens, topk)[:, :, None] == slot_ids[None, None, :], route_weights[:, :, None], 0.0),
+        axis=1,
+    )
+    mixture = mid_float + jnp.einsum(
+        "tso,sow->tw",
+        placed_weights.reshape(tokens, half_cap, owners),
+        returned.astype(jnp.float32),
+        precision=lax.Precision.HIGHEST,
+        preferred_element_type=jnp.float32,
+    )
     final = mixture.astype(jnp.bfloat16)
     return (mid[None], final[None])
 

time: 437 us -> 435 us (level)
  waiting for transfers between devices: 160 us -> 181 us
  Pallas kernels: 29 us -> 12.3 us
  starting transfers between devices: 37.8 us -> 29.6 us
    all_gather x1, waiting for transfers between devices: 0.01 us -> 23.9 us  [body(): lax.all_gather(lax.dynamic_slice_in_dim(out_proj, parity * head_rows, hea...]
    pallas_call x1, Pallas kernels: 29 us -> 12.3 us  [flash_all(): pl.pallas_call(kernel, grid_spec=grid_spec, out_shape=jax.ShapeDtypeStruc...]
    ppermute x1, starting transfers between devices: 30.7 us -> 22.2 us  [body(): partner_cols = lax.ppermute(theirs_cols, 'grp', pair_perm)]
  transfers between devices with their start and end apart: 7 -> 7, of which waited for: 5 -> 4; matrix products, arithmetic and copies ran while one was open for 5% -> 5% of each run, Pallas kernels for 7% -> 3%
where the time goes in v2:
time: 435 us; the launch traced here: 431 us
  waiting for transfers between devices  181 us (42%)
  blocking collectives  98.5 us (23%)
  matrix products  41.8 us (10%)
  local copies, waits for them, and re-layouts  36.5 us (8%)
  starting transfers between devices  29.6 us (7%)
  between operations  22.8 us (5%)
  Pallas kernels  12.3 us (3%)
  other arithmetic  8.17 us (2%)
    all_to_all x1, blocking collectives, body(): lax.all_to_all(split, ('ctx', 'grp'), split_axis=1, concat_axis=1, tiled=...  98.5 us
    all_gather x1, waiting for transfers between devices, body(): kv_all = lax.all_gather(local_kv, 'ctx', axis=0, tiled=False)  78.6 us
    all_to_all x1, waiting for transfers between devices, body(): lax.all_to_all(summed, ('ctx', 'grp'), split_axis=1, concat_axis=1, tiled...  72.6 us
    all_gather x1, waiting for transfers between devices, body(): lax.all_gather(lax.dynamic_slice_in_dim(out_proj, parity * head_rows, hea...  23.9 us
    ppermute x1, starting transfers between devices, body(): partner_cols = lax.ppermute(theirs_cols, 'grp', pair_perm)  22.2 us
    dot_general x2, matrix products, expert_half(): jnp.einsum('sow,wh->soh', rows, in_weights, preferred_element_type=jnp.fl...  15.5 us
    pallas_call x1, Pallas kernels, flash_all(): pl.pallas_call(kernel, grid_spec=grid_spec, out_shape=jax.ShapeDtypeStruc...  12.3 us
    dot_general x2, matrix products, expert_half(): jnp.einsum('soh,hw->sow', hidden, out_weights, preferred_element_type=jnp...  9.59 us
  transfers between devices with their start and end apart: 7, of which 4 were waited for; matrix products, arithmetic and copies ran while one was open for 5% of the time, Pallas kernels for 3%

profile of v2, /device:TPU:1, one launch (start us, length us, event | category | flops | bytes accessed | tf_op | source)
XLA Modules:
  0.0 431.2 jit_solution(2160984578721842208)
XLA Ops:
  7.2 2.2 pad_maximum_fusion.1
  9.8 1.0 copy.117
  11.1 0.7 fusion.60
  20.5 0.7 copy.86
  21.4 2.0 reshape_reshape.8.sink_ref
  23.4 1.3 pad_add_fusion.s_ref
  24.7 78.6 %all-gather.6.cloned.1.call-done = bf16[6144,1024]{1,0:T(8,128)(2,1)} async-done(((bf16[384,1024]{1,0:T(8,128)(2,1)}), bf16[6144,1024]{1,0:T(8,128)(2,1)}) %all-gather.6.cloned.1.call-update) | async-done | bytes 12582928 | tf_op jit(solution)/shard_map/all_gather | solution.py:222
  103.3 12.3 %shard_map.131 = bf16[4,1024,128]{2,1,0:T(8,128)(2,1)S(1)} custom-call(s32[4]{0:T(128)S(1)} %pad_add_fusion.s_ref, bf16[4,1024,128]{2,1,0:T(8,128)(2,1)S(1)} %bitcast.92, s32[128,1]{1,0:T(8,128)S(1)} %iota_add_fusion.qpos_ref, s32[128,1]{1,0:T(8,128)S(1)} %copy.87.qstart_ref, f32[4,1024,1]{2,1,0:T(8,128)S(1)} %reshape_reshape.8.sink_ref, ...), custom_call_target="tpu_custom_call" | custom-call | flops 6442450944 | bytes 8388608 | tf_op jit(solution)/shard_map/pallas_call | solution.py:118
  115.6 1.0 copy-done.2
  116.5 1.5 copy.89
  118.1 0.8 reshape.158
  119.6 22.2 %collective-permute-start = (bf16[128,1024]{0,1:T(8,128)(2,1)S(1)}, bf16[128,1024]{0,1:T(8,128)(2,1)S(1)}, u32[]{:S(2)}, u32[]{:S(2)}) collective-permute-start(bf16[128,1024]{0,1:T(8,128)(2,1)S(1)} %bitcast.103), channel_id=1, source_target_pairs={{0,1},{1,0},{2,3},{3,2},{4,5},{5,4},{6,7},{7,6},{8,9},{9,8},{10,11... | collective-permute-start | bytes 786440 | tf_op jit(solution)/shard_map/ppermute | solution.py:235
  141.8 23.9 %all-gather.4.cloned.1.call-done = bf16[1024,2880]{1,0:T(8,128)(2,1)} async-done(((bf16[64,2880]{1,0:T(8,128)(2,1)}), bf16[1024,2880]{1,0:T(8,128)(2,1)}) %all-gather.4.cloned.1.call-update) | async-done | bytes 5898256 | tf_op jit(solution)/shard_map/all_gather | solution.py:229
  165.7 5.3 %fusion.41 = f32[256,2880]{0,1:T(8,128)S(1)} fusion(bf16[1024,2880]{1,0:T(8,128)(2,1)} %all-gather.4.cloned.1.call-done, bf16[128,1024]{0,1:T(8,128)(2,1)S(1)} %collective-permute-done, bf16[128,1024]{0,1:T(8,128)(2,1)S(1)} %bitcast.102), kind=kOutput, calls=%fused_computation.43 | convolution fusion | flops 1510998016 | bytes 9371648 | tf_op jit(solution)/shard_map/dot_general | solution.py:236
  171.0 1.6 copy-done.5
  172.7 0.8 collective-permute-start.1
  173.8 1.2 reduce-window.19
  176.5 2.0 fusion.28
  178.5 3.1 convolution_convert_fusion
  181.6 8.3 %copy.107 = bf16[5,128,2880]{2,0,1:T(8,128)(2,1)} copy(bf16[5,128,2880]{1,2,0:T(8,128)(2,1)} %convolution_convert_fusion) | data formatting | bytes 7372800 | tf_op jit(solution)/shard_map/convert_element_type | solution.py:271
  189.9 98.5 %all_to_all.10 = bf16[5,128,2880]{2,0,1:T(8,128)(2,1)} all-to-all(bf16[5,128,2880]{2,0,1:T(8,128)(2,1)} %copy.107), channel_id=1, replica_groups=mesh['ctx'=16,'grp'=8] {'ctx','grp'}, dimensions={1} | all-to-all | bytes 7372800 | tf_op jit(solution)/shard_map/all_to_all | solution.py:277
  288.4 7.9 %copy.108 = bf16[5,128,2880]{1,2,0:T(8,128)(2,1)} copy(bf16[5,128,2880]{2,0,1:T(8,128)(2,1)} %all_to_all.10) | data formatting | bytes 7372800 | tf_op jit(solution)/shard_map/all_to_all | solution.py:277
  296.3 1.3 collective-permute-start.2
  297.6 6.3 %collective-permute-done.2 = bf16[5,128,2880]{1,2,0:T(8,128)(2,1)S(1)} collective-permute-done((bf16[5,128,2880]{1,2,0:T(8,128)(2,1)}, bf16[5,128,2880]{1,2,0:T(8,128)(2,1)S(1)}, u32[]{:S(2)}, u32[]{:S(2)}) %collective-permute-start.2) | collective-permute-done | bytes 3686432 | tf_op jit(solution)/shard_map/ppermute | solution.py:278
  303.8 9.2 %fusion = f32[5,128,1536]{2,1,0:T(8,128)S(1)} fusion(bf16[5,128,2880]{1,2,0:T(8,128)(2,1)S(1)} %collective-permute-done.2, bf16[1,2880,1536]{2,1,0:T(8,128)(2,1)} %param.22), kind=kOutput, calls=%fused_computation | convolution fusion | flops 5662310400 | bytes 16465920 | tf_op jit(solution)/shard_map/sow,wh->soh/dot_general | solution.py:281
  313.1 4.1 convolution_convert_fusion.1
  317.7 6.3 %fusion.2 = f32[5,128,1536]{2,1,0:T(8,128)S(1)} fusion(bf16[5,128,2880]{1,2,0:T(8,128)(2,1)S(1)} %copy-done.3, bf16[1,2880,1536]{2,1,0:T(8,128)(2,1)S(1)} %bitcast.107), kind=kOutput, calls=%fused_computation.2 | convolution fusion | flops 5662310400 | bytes 16465920 | tf_op jit(solution)/shard_map/sow,wh->soh/dot_general | solution.py:281
  324.0 5.5 %add_convert_fusion = bf16[5,128,2880]{1,2,0:T(8,128)(2,1)} fusion(bf16[5,128,2880]{1,2,0:T(8,128)(2,1)S(1)} %collective-permute-done.3, bf16[1,768,2880]{1,2,0:T(8,128)(2,1)S(1)} %bitcast.109, f32[5,128,1536]{2,1,0:T(8,128)S(1)} %fusion.2), kind=kOutput, calls=%fused_computation.4 | convolution fusion | flops 2844303360 | bytes 15728640 | tf_op jit(solution)/shard_map/soh,hw->sow/dot_general | solution.py:285
  329.5 8.3 %copy.110 = bf16[5,128,2880]{2,0,1:T(8,128)(2,1)} copy(bf16[5,128,2880]{1,2,0:T(8,128)(2,1)} %add_convert_fusion) | data formatting | bytes 7372800 | tf_op jit(solution)/shard_map/convert_element_type | solution.py:292
  337.8 4.9 %all-to-all-start.1 = ((bf16[5,128,2880]{2,0,1:T(8,128)(2,1)}), bf16[5,128,2880]{2,0,1:T(8,128)(2,1)}, u32[]{:S(2)}, u32[]{:S(2)}) async-start(bf16[5,128,2880]{2,0,1:T(8,128)(2,1)} %copy.110), calls=%async_computation.1 | async-start | bytes 12058624 | tf_op jit(solution)/shard_map/all_to_all | solution.py:293
  343.7 72.6 %all-to-all-done.1 = bf16[5,128,2880]{2,0,1:T(8,128)(2,1)} async-done(((bf16[5,128,2880]{2,0,1:T(8,128)(2,1)}), bf16[5,128,2880]{2,0,1:T(8,128)(2,1)}, u32[]{:S(2)}, u32[]{:S(2)}) %all-to-all-start.1) | async-done | bytes 3686432 | tf_op jit(solution)/shard_map/all_to_all | solution.py:293
  416.4 7.7 %fusion.19 = bf16[1,128,2880]{1,2,0:T(8,128)(2,1)} fusion(f32[128,5,128]{0,2,1:T(8,128)S(1)} %bitcast.99, bf16[5,128,2880]{2,0,1:T(8,128)(2,1)} %all-to-all-done.1, bf16[128,2880]{0,1:T(8,128)(2,1)S(1)} %get-tuple-element.3), kind=kOutput, calls=%fused_computation.15 | convolution fusion | flops 2832261120 | bytes 5488640 | tf_op jit(solution)/shard_map/tso,sow->tw/dot_general | solution.py:299
  (85 shorter events, 5.7 us)
Async XLA Ops:
  7.2 2.3 copy-start
  7.2 3.6 copy-start.11
  7.2 12.7 %copy-start.6 = (bf16[1,128,2048]{2,1,0:T(8,128)(2,1)S(1)}, bf16[1,128,2048]{2,1,0:T(8,128)(2,1)}, u32[]{:S(2)}) copy-start(bf16[1,128,2048]{2,1,0:T(8,128)(2,1)} %param.13) | copy-start | bytes 1572868
  7.2 96.1 %all-gather.6.cloned.1.call-start = ((), (), s32[]{:S(2)}) async-start(), calls=%async_computation.3 | async-start | bytes 13369344 | tf_op jit(solution)/shard_map/all_gather | solution.py:222
  9.4 156.3 %all-gather.4.cloned.1.call-start = ((), (), s32[]{:S(2)}) async-start(), calls=%async_computation.2 | async-start | bytes 6406144 | tf_op jit(solution)/shard_map/all_gather | solution.py:229
  20.2 1.1 copy-start.9
  115.6 1.0 copy-start.2
  119.6 46.1 %collective-permute-start = (bf16[128,1024]{0,1:T(8,128)(2,1)S(1)}, bf16[128,1024]{0,1:T(8,128)(2,1)S(1)}, u32[]{:S(2)}, u32[]{:S(2)}) collective-permute-start(bf16[128,1024]{0,1:T(8,128)(2,1)S(1)} %bitcast.103), channel_id=1, source_target_pairs={{0,1},{1,0},{2,3},{3,2},{4,5},{5,4},{6,7},{7,6},{8,9},{9,8},{10,11... | collective-permute-start | bytes 786440 | tf_op jit(solution)/shard_map/ppermute | solution.py:235
  171.0 1.6 copy-start.5
  172.6 0.9 copy-start.7
  172.7 5.8 %copy-start.8 = (f32[2880]{0:T(1024)S(1)}, f32[2880]{0:T(1024)}, u32[]{:S(2)}) copy-start(f32[2880]{0:T(1024)} %param.19) | copy-start | bytes 34564
  172.7 3.8 collective-permute-start.1
  178.5 237.9 %copy-start.4 = (bf16[128,2880]{0,1:T(8,128)(2,1)}, bf16[128,2880]{0,1:T(8,128)(2,1)S(1)}, u32[]{:S(2)}) copy-start(bf16[128,2880]{0,1:T(8,128)(2,1)S(1)} %get-tuple-element.3) | copy-start | bytes 2211844
  288.4 24.6 %slice-start.3 = ((s8[4423680]{0:T(1024)(128)(4,1)}), s8[229376]{0:T(1024)(128)(4,1)S(1)}, s32[]{:S(2)}) async-start(s8[4423680]{0:T(1024)(128)(4,1)} %bitcast.108), calls=%async_computation.7 | async-start | bytes 458752
  296.3 16.8 %slice-start.4 = ((s8[4423680]{0:T(1024)(128)(4,1)}), s8[4194304]{0:T(1024)(128)(4,1)S(1)}, s32[]{:S(2)}) async-start(s8[4423680]{0:T(1024)(128)(4,1)} %bitcast.108), calls=%async_computation.8 | async-start | bytes 8388608
  296.3 7.5 %collective-permute-start.2 = (bf16[5,128,2880]{1,2,0:T(8,128)(2,1)}, bf16[5,128,2880]{1,2,0:T(8,128)(2,1)S(1)}, u32[]{:S(2)}, u32[]{:S(2)}) collective-permute-start(bf16[5,128,2880]{1,2,0:T(8,128)(2,1)} %copy.108), channel_id=1, source_target_pairs={{0,1},{1,0},{2,3},{3,2},{4,5},{5,4},{6,7},{7,6},{8,9},{9,8},{10,11... | collective-permute-start | bytes 11059208 | tf_op jit(solution)/shard_map/ppermute | solution.py:278
  303.8 13.8 %slice-start = ((s8[8847360]{0:T(1024)(128)(4,1)}), s8[4194304]{0:T(1024)(128)(4,1)S(1)}, s32[]{:S(2)}) async-start(s8[8847360]{0:T(1024)(128)(4,1)} %bitcast.106), calls=%async_computation.4 | async-start | bytes 8388608
  303.8 13.8 %slice-start.1 = ((s8[8847360]{0:T(1024)(128)(4,1)}), s8[4194304]{0:T(1024)(128)(4,1)S(1)}, s32[]{:S(2)}) async-start(s8[8847360]{0:T(1024)(128)(4,1)} %bitcast.106), calls=%async_computation.5 | async-start | bytes 8388608
  313.1 4.6 %copy-start.3 = (bf16[5,128,2880]{1,2,0:T(8,128)(2,1)S(1)}, bf16[5,128,2880]{1,2,0:T(8,128)(2,1)}, u32[]{:S(2)}) copy-start(bf16[5,128,2880]{1,2,0:T(8,128)(2,1)} %copy.108) | copy-start | bytes 11059204
  313.1 4.6 %slice-start.2 = ((s8[8847360]{0:T(1024)(128)(4,1)}), s8[458752]{0:T(1024)(128)(4,1)S(1)}, s32[]{:S(2)}) async-start(s8[8847360]{0:T(1024)(128)(4,1)} %bitcast.106), calls=%async_computation.6 | async-start | bytes 917504
  317.2 6.8 %collective-permute-start.3 = (bf16[5,128,2880]{1,2,0:T(8,128)(2,1)S(1)}, bf16[5,128,2880]{1,2,0:T(8,128)(2,1)S(1)}, u32[]{:S(2)}, u32[]{:S(2)}) collective-permute-start(bf16[5,128,2880]{1,2,0:T(8,128)(2,1)S(1)} %convolution_convert_fusion.1), channel_id=1, source_target_pairs={{0,1},{1,0},{2,3},{3,2},{4,5},{5,4},{6,7},{7,6},{8,9},{9,8},{10,11... | collective-permute-start | bytes 11059208 | tf_op jit(solution)/shard_map/ppermute | solution.py:291
  337.8 4.9 %copy-start.10 = (bf16[2880,64]{0,1:T(8,128)(2,1)S(1)}, bf16[2880,64]{0,1:T(8,128)(2,1)}, u32[]{:S(2)}) copy-start(bf16[2880,64]{0,1:T(8,128)(2,1)} %param.20) | copy-start | bytes 1105924
  337.8 78.6 %all-to-all-start.1 = ((bf16[5,128,2880]{2,0,1:T(8,128)(2,1)}), bf16[5,128,2880]{2,0,1:T(8,128)(2,1)}, u32[]{:S(2)}, u32[]{:S(2)}) async-start(bf16[5,128,2880]{2,0,1:T(8,128)(2,1)} %copy.110), calls=%async_computation.1 | async-start | bytes 12058624 | tf_op jit(solution)/shard_map/all_to_all | solution.py:293
  343.6 80.5 %copy-start.1 = (bf16[128,2880]{0,1:T(8,128)(2,1)S(1)}, bf16[128,2880]{0,1:T(8,128)(2,1)}, u32[]{:S(2)}) copy-start(bf16[128,2880]{0,1:T(8,128)(2,1)} %param.18) | copy-start | bytes 2211844
Sparse Core Ops, SparseCore 0:
  10.2 93.0 all-gather.5
  106.0 59.6 all-gather.3
